TPU v7x, 256 devices: a whole 4x4x8 slice. The times are simulated.
256 devices in a mesh: lon: 16 (over z, core), lat: 16 (over x, y).
Axes of the slice: x: 4, y: 4, z: 8, core: 2. Of those that a mesh axis runs over, the one named last changes fastest.
Arguments:
- state: float32 [16, 512, 4096], P(None, 'lat', 'lon'), may hold values from -6 to 6
- coef_lon: float32 [512, 4096], P('lat', 'lon'), may hold values from 0.2 to 0.24
- coef_lat: float32 [512, 4096], P('lat', 'lon'), may hold values from 0.2 to 0.24
- land_sea: int32 [512, 4096], P('lat', 'lon'), may hold values 0 or 1
- send_cols: int32 [16, 65536], P('lat', 'lon'), may hold values from 0 to 8191
- send_count: int32 [16, 256], P('lat', 'lon'), may hold values from 32 to 256, as said below
- obs_value: float32 [16, 16, 65536], P(None, 'lat', 'lon'), may hold values from -6 to 6
- obs_weight: float32 [16, 16, 65536], P(None, 'lat', 'lon'), may hold values from 0.25 to 4
Outputs:
- increment: float32 [16, 512, 4096], P(None, 'lat', 'lon')
Inputs may be any that keep to these rules, and one draw needn't show every extreme that they name: `send_count`: at most 256 live slots go from one device to one peer; in every latitude band some receiving device gets 256 from every device of the band, which one drawn from the seed. `send_cols`: entries index a column of the sending device's own block, row-major over its 32 x 256 cells.
All inputs are finite; a program needn't handle non-finite values. No bound on the sum of `land_sea` on one device may be relied on, other than what follows from the above.
Results may differ from a plain program's by a relative error of at most 0.00002.
Values sent between devices are 32-bit elements; how exact they have to be, the bound alone decides.
No kernel may reach another device: no remote copies, remote signals or barrier semaphores. Data moves between devices by JAX's collectives and lax.ppermute only.
A program may use at most 64 MiB of HBM per device.

v0:
```python
import jax
import jax.numpy as jnp
from jax import lax
from jax.sharding import PartitionSpec as P

PASSES = 8


def with_halo(block, sides, width):
    for axis, dim in sides:
        count = lax.axis_size(axis)
        forward = [(i, i + 1) for i in range(count - 1)]
        forward.append((count - 1, 0))
        backward = [(target, source) for source, target in forward]
        low = lax.ppermute(
            lax.slice_in_dim(block, block.shape[dim] - width, None, axis=dim), axis, forward
        )
        high = lax.ppermute(lax.slice_in_dim(block, 0, width, axis=dim), axis, backward)
        block = jnp.concatenate([low, block, high], axis=dim)
    return block


def one_pass(layer_field, east_face, north_face):
    flux_east = east_face * (layer_field[:, :, 1:] - layer_field[:, :, :-1])
    flux_north = north_face * (layer_field[:, 1:, :] - layer_field[:, :-1, :])
    return (
        layer_field[:, 1:-1, 1:-1]
        + flux_east[:, 1:-1, 1:]
        - flux_east[:, 1:-1, :-1]
        + flux_north[:, 1:, 1:-1]
        - flux_north[:, :-1, 1:-1]
    )


def body(state, coef_lon, coef_lat, land_sea, send_cols, send_count, obs_value, obs_weight):
    levels, rows_here, cols_here = state.shape
    lon_count = lax.axis_size("lon")
    lat_count = lax.axis_size("lat")
    slots = send_cols.shape[1]
    capacity = slots // lon_count
    columns = state.reshape(levels, rows_here * cols_here)
    targets = send_cols[0]
    slot_index = jnp.arange(slots, dtype=jnp.int32)
    limits = jnp.broadcast_to(send_count[0][:, None], (lon_count, capacity)).reshape(slots)
    usable = jnp.where(slot_index % capacity < limits, 1.0, 0.0).astype(jnp.float32)
    held = jnp.stack([obs_value[:, 0, :], obs_weight[:, 0, :]])
    at_owner = lax.all_to_all(held, "lon", split_axis=2, concat_axis=2, tiled=True)
    at_column = jnp.take(columns, targets, axis=1)
    weighted = at_owner[1] * (at_owner[0] - at_column) * usable
    sea = land_sea.astype(jnp.float32)
    gradient = jnp.zeros((levels, rows_here * cols_here), jnp.float32).at[:, targets].add(weighted)
    gradient = gradient.reshape(levels, rows_here, cols_here) * sea[None]
    rim_width = PASSES
    stacked = jnp.stack([sea, coef_lon, coef_lat])
    padded = with_halo(stacked, (("lon", 2), ("lat", 1)), rim_width)
    lat_index = lax.axis_index("lat")
    row_place = jnp.arange(rows_here + 2 * rim_width, dtype=jnp.int32)
    outside = (row_place < rim_width) & (lat_index == 0) | (row_place >= rows_here + rim_width) & (
        lat_index == lat_count - 1
    )
    inside = jnp.where(outside, 0.0, 1.0).astype(jnp.float32)[:, None]
    sea_rim = padded[0] * inside
    east_face = padded[1][:, :-1] * sea_rim[:, :-1] * sea_rim[:, 1:]
    north_face = padded[2][:-1, :] * sea_rim[:-1, :] * sea_rim[1:, :]
    field = with_halo(gradient, (("lon", 2), ("lat", 1)), rim_width)
    for step_number in range(PASSES):
        high, wide = (field.shape[1], field.shape[2])
        field = one_pass(
            field,
            east_face[step_number : step_number + high, step_number : step_number + wide - 1],
            north_face[step_number : step_number + high - 1, step_number : step_number + wide],
        )
    gradient = field
    return gradient


def solution(mesh):
    placed = (
        P(None, "lat", "lon"),
        P("lat", "lon"),
        P("lat", "lon"),
        P("lat", "lon"),
        P("lat", "lon"),
        P("lat", "lon"),
        P(None, "lat", "lon"),
        P(None, "lat", "lon"),
    )
    return jax.shard_map(
        body, mesh=mesh, in_specs=placed, out_specs=P(None, "lat", "lon"), check_vma=False
    )
```

profile of v0, /device:TPU:32, one launch (start us, length us, event | category | flops | bytes accessed | tf_op | source)
XLA Modules:
  0.0 152.6 jit_solution(4161188813281966988)
XLA Ops:
  0.0 1.3 copy_bitcast_fusion
  1.4 4.4 %copy.17 = f32[2,16,4096]{1,0,2:T(2,128)} copy(f32[2,16,4096]{2,1,0:T(8,128)S(1)} %pad_maximum_fusion.1) | data formatting | bytes 1048576 | tf_op jit(solution)/shard_map/stack | solution.py:46
  5.8 8.0 %reshape.116 = f32[16,1,8192]{2,1,0:T(1,128)} reshape(f32[4096,2,16]{2,1,0:T(2,128)} %bitcast.49) | data formatting | bytes 1048576
  13.7 8.7 %all-to-all-start = ((f32[16,1,8192]{2,1,0:T(1,128)}), f32[16,1,8192]{2,1,0:T(1,128)S(1)}, u32[]{:S(2)}, u32[]{:S(2)}) async-start(f32[16,1,8192]{2,1,0:T(1,128)} %reshape.116), calls=%async_computation | async-start | bytes 1048576 | tf_op jit(solution)/shard_map/all_to_all | solution.py:47
  22.6 0.1 collective-permute-start.5
  22.7 0.4 collective-permute-start.4
  23.3 11.7 %collective-permute-done.5 = f32[3,32,8]{2,1,0:T(8,128)S(1)} collective-permute-done((f32[3,32,8]{2,1,0:T(8,128)S(1)}, f32[3,32,8]{2,1,0:T(8,128)S(1)}, u32[]{:S(2)}, u32[]{:S(2)}) %collective-permute-start.5) | collective-permute-done | bytes 3104 | tf_op jit(solution)/shard_map/ppermute | solution.py:18
  35.0 0.1 pad_maximum_fusion.11
  35.1 5.3 %collective-permute-start.7 = (f32[3,8,272]{2,1,0:T(8,128)S(1)}, f32[3,8,272]{2,1,0:T(8,128)S(1)}, u32[]{:S(2)}, u32[]{:S(2)}) collective-permute-start(f32[3,8,272]{2,1,0:T(8,128)S(1)} %get-tuple-element.12), channel_id=1, source_target_pairs={{1,0},{2,1},{3,2},{4,3},{5,4},{6,5},{7,6},{8,7},{9,8},{10,9},{11,1... | collective-permute-start | bytes 78344 | tf_op jit(solution)/shard_map/ppermute | solution.py:18
  40.4 2.6 %copy.20 = f32[16,32,256]{0,2,1:T(8,128)} copy(f32[16,32,256]{2,1,0:T(8,128)S(1)} %copy-done.1) | data formatting | bytes 1048576 | tf_op args[0]
  43.1 4.6 %collective-permute-done.6 = f32[3,8,272]{2,1,0:T(8,128)S(1)} collective-permute-done((f32[3,8,272]{2,1,0:T(8,128)S(1)}, f32[3,8,272]{2,1,0:T(8,128)S(1)}, u32[]{:S(2)}, u32[]{:S(2)}) %collective-permute-start.6) | collective-permute-done | bytes 26144 | tf_op jit(solution)/shard_map/ppermute | solution.py:15
  47.7 0.1 pad_maximum_fusion.2
  47.9 0.5 broadcast.109
  48.4 1.9 %reduce = f32[16,8192]{1,0:T(8,128)S(1)} reduce(f32[16,1,8192]{2,1,0:T(1,128)S(1)} %all-to-all-done, f32[]{:T(128)} %broadcast.109), dimensions={1}, to_apply=%all_to_all.3.reduce_sub_computation | reduce | bytes 1048580 | tf_op jit(solution)/shard_map/all_to_all | solution.py:47
  50.3 7.0 %reshape.117 = f32[4096,2,16]{2,1,0:T(2,128)} reshape(f32[16,8192]{1,0:T(8,128)S(1)} %reduce) | data formatting | bytes 1048576
  57.3 7.6 %fusion.33 = (f32[1,16,4096]{1,0,2:T(1,128)S(1)}, f32[1,16,4096]{1,0,2:T(1,128)}) fusion(f32[2,16,4096]{1,0,2:T(2,128)} %bitcast.52), kind=kLoop, calls=%fused_computation.114 | loop fusion | bytes 1048576 | tf_op jit(solution)/shard_map/slice | solution.py:49
  64.9 51.2 %scatter_custom_fusion = f32[16,8192]{0,1:T(8,128)} fusion(s32[4096]{0:T(1024)S(1)} %bitcast.63, f32[16,4096]{0,1:T(8,128)} %bitcast.54, f32[16,4096]{0,1:T(8,128)S(1)} %bitcast.53, f32[]{:T(128)} %constant.19.clone.1, f32[]{:T(128)} %constant.23.clone.1, f32[4096]{0:T(1024)S(1)} %fusion.31, pred[4096]{0:T(1024)(128)(4,1)S(1)} %compare_and_fusion, ...), kind=kCustom, calls=%fused_computation.2 | custom fusion | flops 327680 | bytes 3444744 | tf_op jit(solution)/shard_map/scatter-add | solution.py:51
  116.1 2.9 %copy.21 = f32[16,32,256]{2,1,0:T(8,128)S(1)} copy(f32[16,32,256]{0,2,1:T(8,128)} %bitcast.51) | data formatting | bytes 1048576 | tf_op jit(solution)/shard_map/reshape | solution.py:52
  119.1 0.1 fusion.34
  119.2 0.8 collective-permute-start.1
  120.0 0.1 slice.453
  120.1 0.1 slice.464
  120.2 3.7 %collective-permute-done.1 = f32[16,32,8]{2,1,0:T(8,128)S(1)} collective-permute-done((f32[16,32,8]{2,1,0:T(8,128)S(1)}, f32[16,32,8]{2,1,0:T(8,128)S(1)}, u32[]{:S(2)}, u32[]{:S(2)}) %collective-permute-start.1) | collective-permute-done | bytes 16416 | tf_op jit(solution)/shard_map/ppermute | solution.py:18
  123.9 2.6 %collective-permute-done = f32[16,32,8]{2,1,0:T(8,128)S(1)} collective-permute-done((f32[16,32,8]{2,1,0:T(8,128)S(1)}, f32[16,32,8]{2,1,0:T(8,128)S(1)}, u32[]{:S(2)}, u32[]{:S(2)}) %collective-permute-start) | collective-permute-done | bytes 16416 | tf_op jit(solution)/shard_map/ppermute | solution.py:15
  126.5 0.2 pad_maximum_fusion.5
  126.7 0.9 collective-permute-start.3
  127.6 1.2 collective-permute-start.2
  128.8 0.1 slice_multiply_fusion.2
  128.9 0.1 slice.448
  129.0 0.1 slice.459
  129.0 0.1 slice.475
  129.1 0.1 slice.470
  129.2 0.1 slice.486
  129.3 0.1 slice.481
  129.4 0.1 slice.497
  129.5 0.1 slice.492
  129.6 0.1 slice.508
  129.9 3.0 %collective-permute-done.3 = f32[16,8,272]{2,1,0:T(8,128)S(1)} collective-permute-done((f32[16,8,272]{2,1,0:T(8,128)S(1)}, f32[16,8,272]{2,1,0:T(8,128)S(1)}, u32[]{:S(2)}, u32[]{:S(2)}) %collective-permute-start.3) | collective-permute-done | bytes 139296 | tf_op jit(solution)/shard_map/ppermute | solution.py:18
  132.9 4.6 %collective-permute-done.2 = f32[16,8,272]{2,1,0:T(8,128)S(1)} collective-permute-done((f32[16,8,272]{2,1,0:T(8,128)S(1)}, f32[16,8,272]{2,1,0:T(8,128)S(1)}, u32[]{:S(2)}, u32[]{:S(2)}) %collective-permute-start.2) | collective-permute-done | bytes 139296 | tf_op jit(solution)/shard_map/ppermute | solution.py:15
  137.5 0.3 pad_maximum_fusion
  137.9 0.2 fusion.13
  138.0 0.4 fusion.14
  138.4 1.4 slice_subtract_fusion.10
  139.9 0.2 fusion.11
  140.0 0.4 fusion.12
  140.4 1.4 slice_subtract_fusion.6
  141.9 0.2 fusion.9
  142.0 0.4 fusion.10
  142.4 1.4 slice_subtract_fusion.2
  143.9 0.2 fusion.7
  144.0 0.4 fusion.8
  144.4 1.2 slice_subtract_fusion.28
  145.6 0.1 fusion.24
  145.7 0.3 fusion.25
  146.1 1.2 slice_subtract_fusion.24
  147.3 0.1 fusion.22
  147.4 0.3 fusion.23
  147.8 1.2 slice_subtract_fusion.20
  149.0 0.1 fusion.20
  149.1 0.3 fusion.21
  149.4 1.2 slice_subtract_fusion.16
  150.6 0.1 fusion.18
  150.8 0.3 fusion.19
  151.1 1.5 slice_subtract_fusion.30
  (35 shorter events, 0.7 us)
Async XLA Ops:
  0.0 23.1 %copy-start = (s32[1,16]{1,0:T(1,128)S(1)}, s32[1,16]{1,0:T(1,128)}, u32[]{:S(2)}) copy-start(s32[1,16]{1,0:T(1,128)} %param.13) | copy-start | bytes 196
  5.8 16.7 %copy-start.5 = (s32[32,256]{1,0:T(8,128)S(1)}, s32[32,256]{1,0:T(8,128)}, u32[]{:S(2)}) copy-start(s32[32,256]{1,0:T(8,128)} %param.11) | copy-start | bytes 98308
  5.8 16.7 %copy-start.2 = (f32[32,256]{1,0:T(8,128)S(1)}, f32[32,256]{1,0:T(8,128)}, u32[]{:S(2)}) copy-start(f32[32,256]{1,0:T(8,128)} %param.10) | copy-start | bytes 98308
  5.8 16.7 %copy-start.3 = (f32[32,256]{1,0:T(8,128)S(1)}, f32[32,256]{1,0:T(8,128)}, u32[]{:S(2)}) copy-start(f32[32,256]{1,0:T(8,128)} %param.9) | copy-start | bytes 98308
  13.7 9.4 %copy-start.4 = (s32[1,4096]{1,0:T(1,128)S(1)}, s32[1,4096]{1,0:T(1,128)}, u32[]{:S(2)}) copy-start(s32[1,4096]{1,0:T(1,128)} %param.12) | copy-start | bytes 49156
  13.7 26.7 %copy-start.1 = (f32[16,32,256]{2,1,0:T(8,128)S(1)}, f32[16,32,256]{2,1,0:T(8,128)}, u32[]{:S(2)}) copy-start(f32[16,32,256]{2,1,0:T(8,128)} %param.8) | copy-start | bytes 1572868
  13.7 34.2 %all-to-all-start = ((f32[16,1,8192]{2,1,0:T(1,128)}), f32[16,1,8192]{2,1,0:T(1,128)S(1)}, u32[]{:S(2)}, u32[]{:S(2)}) async-start(f32[16,1,8192]{2,1,0:T(1,128)} %reshape.116), calls=%async_computation | async-start | bytes 1048576 | tf_op jit(solution)/shard_map/all_to_all | solution.py:47
  22.6 12.4 %collective-permute-start.5 = (f32[3,32,8]{2,1,0:T(8,128)S(1)}, f32[3,32,8]{2,1,0:T(8,128)S(1)}, u32[]{:S(2)}, u32[]{:S(2)}) collective-permute-start(f32[3,32,8]{2,1,0:T(8,128)S(1)} %get-tuple-element.14), channel_id=1, source_target_pairs={{16,0},{32,16},{48,32},{64,48},{80,64},{96,80},{112,96},{128,112},... | collective-permute-start | bytes 9224 | tf_op jit(solution)/shard_map/ppermute | solution.py:18
  22.7 12.3 %collective-permute-start.4 = (f32[3,32,8]{2,1,0:T(8,128)S(1)}, f32[3,32,8]{2,1,0:T(8,128)S(1)}, u32[]{:S(2)}, u32[]{:S(2)}) collective-permute-start(f32[3,32,8]{2,1,0:T(8,128)S(1)} %get-tuple-element.13), channel_id=1, source_target_pairs={{0,16},{16,32},{32,48},{48,64},{64,80},{80,96},{96,112},{112,128},... | collective-permute-start | bytes 9224 | tf_op jit(solution)/shard_map/ppermute | solution.py:15
  35.1 8.0 %collective-permute-start.7 = (f32[3,8,272]{2,1,0:T(8,128)S(1)}, f32[3,8,272]{2,1,0:T(8,128)S(1)}, u32[]{:S(2)}, u32[]{:S(2)}) collective-permute-start(f32[3,8,272]{2,1,0:T(8,128)S(1)} %get-tuple-element.12), channel_id=1, source_target_pairs={{1,0},{2,1},{3,2},{4,3},{5,4},{6,5},{7,6},{8,7},{9,8},{10,9},{11,1... | collective-permute-start | bytes 78344 | tf_op jit(solution)/shard_map/ppermute | solution.py:18
  40.4 7.3 %collective-permute-start.6 = (f32[3,8,272]{2,1,0:T(8,128)S(1)}, f32[3,8,272]{2,1,0:T(8,128)S(1)}, u32[]{:S(2)}, u32[]{:S(2)}) collective-permute-start(f32[3,8,272]{2,1,0:T(8,128)S(1)} %get-tuple-element.11), channel_id=1, source_target_pairs={{0,1},{1,2},{2,3},{3,4},{4,5},{5,6},{6,7},{7,8},{8,9},{9,10},{10,1... | collective-permute-start | bytes 78344 | tf_op jit(solution)/shard_map/ppermute | solution.py:15
  119.2 4.7 %collective-permute-start.1 = (f32[16,32,8]{2,1,0:T(8,128)S(1)}, f32[16,32,8]{2,1,0:T(8,128)S(1)}, u32[]{:S(2)}, u32[]{:S(2)}) collective-permute-start(f32[16,32,8]{2,1,0:T(8,128)S(1)} %get-tuple-element.10), channel_id=1, source_target_pairs={{16,0},{32,16},{48,32},{64,48},{80,64},{96,80},{112,96},{128,112},... | collective-permute-start | bytes 49160 | tf_op jit(solution)/shard_map/ppermute | solution.py:18
  120.0 6.5 %collective-permute-start = (f32[16,32,8]{2,1,0:T(8,128)S(1)}, f32[16,32,8]{2,1,0:T(8,128)S(1)}, u32[]{:S(2)}, u32[]{:S(2)}) collective-permute-start(f32[16,32,8]{2,1,0:T(8,128)S(1)} %get-tuple-element.9), channel_id=1, source_target_pairs={{0,16},{16,32},{32,48},{48,64},{64,80},{80,96},{96,112},{112,128},... | collective-permute-start | bytes 49160 | tf_op jit(solution)/shard_map/ppermute | solution.py:15
  126.7 6.2 %collective-permute-start.3 = (f32[16,8,272]{2,1,0:T(8,128)S(1)}, f32[16,8,272]{2,1,0:T(8,128)S(1)}, u32[]{:S(2)}, u32[]{:S(2)}) collective-permute-start(f32[16,8,272]{2,1,0:T(8,128)S(1)} %get-tuple-element.8), channel_id=1, source_target_pairs={{1,0},{2,1},{3,2},{4,3},{5,4},{6,5},{7,6},{8,7},{9,8},{10,9},{11,1... | collective-permute-start | bytes 417800 | tf_op jit(solution)/shard_map/ppermute | solution.py:18
  127.6 10.0 %collective-permute-start.2 = (f32[16,8,272]{2,1,0:T(8,128)S(1)}, f32[16,8,272]{2,1,0:T(8,128)S(1)}, u32[]{:S(2)}, u32[]{:S(2)}) collective-permute-start(f32[16,8,272]{2,1,0:T(8,128)S(1)} %get-tuple-element.7), channel_id=1, source_target_pairs={{0,1},{1,2},{2,3},{3,4},{4,5},{5,6},{6,7},{7,8},{8,9},{9,10},{10,1... | collective-permute-start | bytes 417800 | tf_op jit(solution)/shard_map/ppermute | solution.py:15
where the time goes:
time: 153 us
  other arithmetic  68.8 us (45%)
  local copies, waits for them, and re-layouts  35.8 us (23%)
  waiting for transfers between devices  30.2 us (20%)
  starting transfers between devices  17.4 us (11%)
    scatter-add x1, other arithmetic, body(): jnp.zeros((levels, rows_here * cols_here), jnp.float32).at[:, targets]  51.2 us
    unnamed x18, local copies, waits for them, and re-layouts  19 us
    ppermute x4, waiting for transfers between devices, with_halo(): lax.ppermute(lax.slice_in_dim(block, 0, width, axis=dim), axis, backward)  18.4 us
    ppermute x4, waiting for transfers between devices, with_halo(): lax.ppermute(lax.slice_in_dim(block, block.shape[dim] - width, None, axis...  11.8 us
    sub x8, other arithmetic, one_pass(): layer_field[:, 1:-1, 1:-1] + flux_east[:, 1:-1, 1:]  10.6 us
    all_to_all x1, starting transfers between devices, body(): lax.all_to_all(held, 'lon', split_axis=2, concat_axis=2, tiled=True)  8.72 us
    slice x1, local copies, waits for them, and re-layouts, body(): weighted = at_owner[1] * (at_owner[0] - at_column) * usable  7.62 us
    ppermute x4, starting transfers between devices, with_halo(): lax.ppermute(lax.slice_in_dim(block, 0, width, axis=dim), axis, backward)  7.1 us
  transfers between devices with their start and end apart: 9, of which 6 were waited for; matrix products, arithmetic and copies ran while one was open for 3% of the time, Pallas kernels for 0%

commit v1 on v0

--- a/solution.py
+++ b/solution.py
@@ -44,7 +44,10 @@
     limits = jnp.broadcast_to(send_count[0][:, None], (lon_count, capacity)).reshape(slots)
     usable = jnp.where(slot_index % capacity < limits, 1.0, 0.0).astype(jnp.float32)
     held = jnp.stack([obs_value[:, 0, :], obs_weight[:, 0, :]])
-    at_owner = lax.all_to_all(held, "lon", split_axis=2, concat_axis=2, tiled=True)
+    at_owner = jnp.concatenate(
+        lax.all_to_all(jnp.stack(jnp.split(held, lax.axis_size("lon"), axis=2)), "lon", 0, 0),
+        axis=2,
+    )
     at_column = jnp.take(columns, targets, axis=1)
     weighted = at_owner[1] * (at_owner[0] - at_column) * usable
     sea = land_sea.astype(jnp.float32)

time: 153 us -> 134 us (0.88)
  the two profiles are of different devices: /device:TPU:32 before, /device:TPU:30 now
where the time goes in v1:
time: 134 us; the launch traced here: 133 us
  other arithmetic  78.8 us (59%)
  waiting for transfers between devices  25.3 us (19%)
  starting transfers between devices  18.7 us (14%)
  local copies, waits for them, and re-layouts  10 us (7%)
    scatter-add x1, other arithmetic, body(): jnp.zeros((levels, rows_here * cols_here), jnp.float32).at[:, targets]  51.3 us
    ppermute x4, waiting for transfers between devices, with_halo(): lax.ppermute(lax.slice_in_dim(block, block.shape[dim] - width, None, axis...  18.6 us
    unnamed x15, other arithmetic  11.3 us
    sub x8, other arithmetic, one_pass(): layer_field[:, 1:-1, 1:-1] + flux_east[:, 1:-1, 1:]  10.6 us
    ppermute x4, starting transfers between devices, with_halo(): lax.ppermute(lax.slice_in_dim(block, 0, width, axis=dim), axis, backward)  8.7 us
    all_to_all x1, starting transfers between devices, body(): lax.all_to_all(jnp.stack(jnp.split(held, lax.axis_size('lon'), axis=2)),...  8.57 us
    ppermute x4, waiting for transfers between devices, with_halo(): lax.ppermute(lax.slice_in_dim(block, 0, width, axis=dim), axis, backward)  6.78 us
    slice x3, local copies, waits for them, and re-layouts, body(): weighted = at_owner[1] * (at_owner[0] - at_column) * usable  3.06 us
  transfers between devices with their start and end apart: 9, of which 5 were waited for; matrix products, arithmetic and copies ran while one was open for 3% of the time, Pallas kernels for 0%

profile of v1, /device:TPU:30, one launch (start us, length us, event | category | flops | bytes accessed | tf_op | source)
XLA Modules:
  0.0 133.3 jit_solution(4822688152803268491)
XLA Ops:
  0.0 1.4 %constant_dynamic-update-slice_fusion.14 = f32[16,2,16,256]{3,1,2,0:T(2,128)} fusion(f32[1,16,4096]{2,0,1:T(1,128)} %bitcast.76, f32[1,16,4096]{2,0,1:T(1,128)} %bitcast.92), kind=kLoop, calls=%fused_computation.160 | loop fusion | flops 8191 | bytes 557056
  1.5 1.4 %constant_dynamic-update-slice_fusion.13 = f32[16,2,16,256]{3,1,2,0:T(2,128)} fusion(f32[16,2,16,256]{3,1,2,0:T(2,128)} %constant_dynamic-update-slice_fusion.14, f32[1,16,4096]{2,0,1:T(1,128)} %bitcast.77, f32[1,16,4096]{2,0,1:T(1,128)} %bitcast.93), kind=kLoop, calls=%fused_computation.159 | loop fusion | flops 8192 | bytes 557056
  2.8 0.7 constant_dynamic-update-slice_fusion.12
  3.5 0.6 constant_dynamic-update-slice_fusion.11
  4.1 0.6 constant_dynamic-update-slice_fusion.10
  4.8 0.6 constant_dynamic-update-slice_fusion.9
  5.4 0.6 constant_dynamic-update-slice_fusion.8
  6.1 0.6 constant_dynamic-update-slice_fusion.7
  6.7 0.6 constant_dynamic-update-slice_fusion.6
  7.4 0.6 constant_dynamic-update-slice_fusion.5
  8.0 0.6 constant_dynamic-update-slice_fusion.4
  8.7 0.6 constant_dynamic-update-slice_fusion.3
  9.3 0.6 constant_dynamic-update-slice_fusion.2
  10.0 0.6 constant_dynamic-update-slice_fusion.1
  10.6 0.6 constant_dynamic-update-slice_fusion
  11.3 0.6 fusion.43
  12.0 8.6 %all-to-all-start = ((f32[16,2,16,256]{3,1,2,0:T(2,128)}), f32[16,2,16,256]{3,1,2,0:T(2,128)S(1)}, u32[]{:S(2)}, u32[]{:S(2)}) async-start(f32[16,2,16,256]{3,1,2,0:T(2,128)} %fusion.43), calls=%async_computation | async-start | bytes 1048576 | tf_op jit(solution)/shard_map/all_to_all | solution.py:48
  20.7 0.4 collective-permute-start.4
  21.1 2.6 %collective-permute-start.5 = (f32[3,32,8]{2,1,0:T(8,128)S(1)}, f32[3,32,8]{2,1,0:T(8,128)S(1)}, u32[]{:S(2)}, u32[]{:S(2)}) collective-permute-start(f32[3,32,8]{2,1,0:T(8,128)S(1)} %get-tuple-element.14), channel_id=1, source_target_pairs={{16,0},{32,16},{48,32},{64,48},{80,64},{96,80},{112,96},{128,112},... | collective-permute-start | bytes 9224 | tf_op jit(solution)/shard_map/ppermute | solution.py:18
  23.8 12.2 %collective-permute-done.4 = f32[3,32,8]{2,1,0:T(8,128)S(1)} collective-permute-done((f32[3,32,8]{2,1,0:T(8,128)S(1)}, f32[3,32,8]{2,1,0:T(8,128)S(1)}, u32[]{:S(2)}, u32[]{:S(2)}) %collective-permute-start.4) | collective-permute-done | bytes 3104 | tf_op jit(solution)/shard_map/ppermute | solution.py:15
  36.0 0.1 pad_maximum_fusion.10
  36.1 0.2 collective-permute-start.6
  36.3 1.9 %collective-permute-start.7 = (f32[3,8,272]{2,1,0:T(8,128)S(1)}, f32[3,8,272]{2,1,0:T(8,128)S(1)}, u32[]{:S(2)}, u32[]{:S(2)}) collective-permute-start(f32[3,8,272]{2,1,0:T(8,128)S(1)} %get-tuple-element.12), channel_id=1, source_target_pairs={{1,0},{2,1},{3,2},{4,3},{5,4},{6,5},{7,6},{8,7},{9,8},{10,9},{11,1... | collective-permute-start | bytes 78344 | tf_op jit(solution)/shard_map/ppermute | solution.py:18
  38.2 2.6 %copy.15 = f32[16,32,256]{0,2,1:T(8,128)} copy(f32[16,32,256]{2,1,0:T(8,128)S(1)} %copy-done.3) | data formatting | bytes 1048576 | tf_op args[0]
  40.9 2.8 %collective-permute-done.7 = f32[3,8,272]{2,1,0:T(8,128)S(1)} collective-permute-done((f32[3,8,272]{2,1,0:T(8,128)S(1)}, f32[3,8,272]{2,1,0:T(8,128)S(1)}, u32[]{:S(2)}, u32[]{:S(2)}) %collective-permute-start.7) | collective-permute-done | bytes 26144 | tf_op jit(solution)/shard_map/ppermute | solution.py:18
  43.6 0.1 pad_maximum_fusion.1
  43.8 0.5 fusion.51
  44.4 0.7 copy.13
  45.1 1.8 %copy.14 = f32[1,16,16,256]{1,3,2,0:T(8,128)} copy(f32[1,16,16,256]{3,0,1,2:T(1,128)S(1)} %get-tuple-element.9) | data formatting | bytes 524288 | tf_op jit(solution)/shard_map/slice | solution.py:52
  46.9 51.3 %scatter_custom_fusion = f32[16,8192]{0,1:T(8,128)} fusion(s32[4096]{0:T(1024)S(1)} %bitcast.121, f32[16,4096]{0,1:T(8,128)S(1)} %bitcast.110, f32[16,4096]{0,1:T(8,128)} %bitcast.111, f32[]{:T(128)} %constant.19.clone.1, f32[]{:T(128)} %constant.23.clone.1, f32[4096]{0:T(1024)S(1)} %fusion.48, pred[4096]{0:T(1024)(128)(4,1)S(1)} %compare_and_fusion, ...), kind=kCustom, calls=%fused_computation.2 | custom fusion | flops 327680 | bytes 3444744 | tf_op jit(solution)/shard_map/scatter-add | solution.py:54
  98.2 2.9 %copy.16 = f32[16,32,256]{2,1,0:T(8,128)S(1)} copy(f32[16,32,256]{0,2,1:T(8,128)} %bitcast.109) | data formatting | bytes 1048576 | tf_op jit(solution)/shard_map/reshape | solution.py:55
  101.1 0.1 fusion.50
  101.3 2.9 %collective-permute-start.1 = (f32[16,32,8]{2,1,0:T(8,128)S(1)}, f32[16,32,8]{2,1,0:T(8,128)S(1)}, u32[]{:S(2)}, u32[]{:S(2)}) collective-permute-start(f32[16,32,8]{2,1,0:T(8,128)S(1)} %get-tuple-element.8), channel_id=1, source_target_pairs={{16,0},{32,16},{48,32},{64,48},{80,64},{96,80},{112,96},{128,112},... | collective-permute-start | bytes 49160 | tf_op jit(solution)/shard_map/ppermute | solution.py:18
  104.5 3.8 %collective-permute-done = f32[16,32,8]{2,1,0:T(8,128)S(1)} collective-permute-done((f32[16,32,8]{2,1,0:T(8,128)S(1)}, f32[16,32,8]{2,1,0:T(8,128)S(1)}, u32[]{:S(2)}, u32[]{:S(2)}) %collective-permute-start) | collective-permute-done | bytes 16416 | tf_op jit(solution)/shard_map/ppermute | solution.py:15
  108.3 0.2 pad_maximum_fusion.4
  108.5 0.8 collective-permute-start.2
  109.3 1.3 collective-permute-start.3
  111.7 2.6 %collective-permute-done.2 = f32[16,8,272]{2,1,0:T(8,128)S(1)} collective-permute-done((f32[16,8,272]{2,1,0:T(8,128)S(1)}, f32[16,8,272]{2,1,0:T(8,128)S(1)}, u32[]{:S(2)}, u32[]{:S(2)}) %collective-permute-start.2) | collective-permute-done | bytes 139296 | tf_op jit(solution)/shard_map/ppermute | solution.py:15
  114.2 4.0 %collective-permute-done.3 = f32[16,8,272]{2,1,0:T(8,128)S(1)} collective-permute-done((f32[16,8,272]{2,1,0:T(8,128)S(1)}, f32[16,8,272]{2,1,0:T(8,128)S(1)}, u32[]{:S(2)}, u32[]{:S(2)}) %collective-permute-start.3) | collective-permute-done | bytes 139296 | tf_op jit(solution)/shard_map/ppermute | solution.py:18
  118.3 0.3 pad_maximum_fusion
  118.6 0.4 fusion.14
  119.0 0.2 fusion.13
  119.2 1.4 %slice_subtract_fusion.10 = f32[16,46,270]{2,1,0:T(8,128)S(1)} fusion(f32[16,47,272]{2,1,0:T(8,128)S(1)} %fusion.13, f32[16,48,271]{2,1,0:T(8,128)S(1)} %fusion.14, f32[16,48,272]{2,1,0:T(8,128)S(1)} %pad_maximum_fusion), kind=kLoop, calls=%fused_computation.29 | loop fusion | flops 794880 | bytes 4769280 | tf_op jit(solution)/shard_map/sub | solution.py:27
  120.6 0.4 fusion.12
  121.0 0.2 fusion.11
  121.1 1.4 %slice_subtract_fusion.6 = f32[16,44,268]{2,1,0:T(8,128)S(1)} fusion(f32[16,45,270]{2,1,0:T(8,128)S(1)} %fusion.11, f32[16,46,269]{2,1,0:T(8,128)S(1)} %fusion.12, f32[16,46,270]{2,1,0:T(8,128)S(1)} %slice_subtract_fusion.10), kind=kLoop, calls=%fused_computation.21 | loop fusion | flops 754688 | bytes 4528128 | tf_op jit(solution)/shard_map/sub | solution.py:27
  122.6 0.4 fusion.10
  123.0 0.2 fusion.9
  123.1 1.4 %slice_subtract_fusion.2 = f32[16,42,266]{2,1,0:T(8,128)S(1)} fusion(f32[16,43,268]{2,1,0:T(8,128)S(1)} %fusion.9, f32[16,44,267]{2,1,0:T(8,128)S(1)} %fusion.10, f32[16,44,268]{2,1,0:T(8,128)S(1)} %slice_subtract_fusion.6), kind=kLoop, calls=%fused_computation.13 | loop fusion | flops 715008 | bytes 4290048 | tf_op jit(solution)/shard_map/sub | solution.py:27
  124.6 0.4 fusion.8
  125.0 0.2 fusion.7
  125.1 1.2 slice_subtract_fusion.28
  126.3 0.3 fusion.25
  126.7 0.1 fusion.24
  126.8 1.2 slice_subtract_fusion.24
  128.0 0.3 fusion.23
  128.4 0.1 fusion.22
  128.5 1.2 slice_subtract_fusion.20
  129.7 0.3 fusion.21
  130.0 0.1 fusion.20
  130.2 1.2 slice_subtract_fusion.16
  131.4 0.3 fusion.19
  131.7 0.1 fusion.18
  131.9 1.5 %slice_subtract_fusion.30 = f32[16,32,256]{2,1,0:T(8,128)} fusion(f32[16,33,258]{2,1,0:T(8,128)S(1)} %fusion.18, f32[16,34,257]{2,1,0:T(8,128)S(1)} %fusion.19, f32[16,34,258]{2,1,0:T(8,128)S(1)} %slice_subtract_fusion.16), kind=kLoop, calls=%fused_computation.103 | loop fusion | flops 524288 | bytes 3145728 | tf_op jit(solution)/shard_map/sub | solution.py:27
  (50 shorter events, 1.7 us)
Async XLA Ops:
  0.0 23.7 %copy-start = (s32[1,16]{1,0:T(1,128)S(1)}, s32[1,16]{1,0:T(1,128)}, u32[]{:S(2)}) copy-start(s32[1,16]{1,0:T(1,128)} %param.13) | copy-start | bytes 196
  0.0 2.8 %copy-start.2 = (f32[16,1,4096]{2,1,0:T(1,128)S(1)}, f32[16,1,4096]{2,1,0:T(1,128)}, u32[]{:S(2)}) copy-start(f32[16,1,4096]{2,1,0:T(1,128)} %param.14) | copy-start | bytes 786436
  0.0 2.8 %copy-start.1 = (f32[16,1,4096]{2,1,0:T(1,128)S(1)}, f32[16,1,4096]{2,1,0:T(1,128)}, u32[]{:S(2)}) copy-start(f32[16,1,4096]{2,1,0:T(1,128)} %param.15) | copy-start | bytes 786436
  10.6 9.9 %copy-start.7 = (s32[32,256]{1,0:T(8,128)S(1)}, s32[32,256]{1,0:T(8,128)}, u32[]{:S(2)}) copy-start(s32[32,256]{1,0:T(8,128)} %param.11) | copy-start | bytes 98308
  10.6 9.9 %copy-start.4 = (f32[32,256]{1,0:T(8,128)S(1)}, f32[32,256]{1,0:T(8,128)}, u32[]{:S(2)}) copy-start(f32[32,256]{1,0:T(8,128)} %param.10) | copy-start | bytes 98308
  10.6 9.9 %copy-start.5 = (f32[32,256]{1,0:T(8,128)S(1)}, f32[32,256]{1,0:T(8,128)}, u32[]{:S(2)}) copy-start(f32[32,256]{1,0:T(8,128)} %param.9) | copy-start | bytes 98308
  11.3 12.3 %copy-start.6 = (s32[1,4096]{1,0:T(1,128)S(1)}, s32[1,4096]{1,0:T(1,128)}, u32[]{:S(2)}) copy-start(s32[1,4096]{1,0:T(1,128)} %param.12) | copy-start | bytes 49156
  11.3 26.9 %copy-start.3 = (f32[16,32,256]{2,1,0:T(8,128)S(1)}, f32[16,32,256]{2,1,0:T(8,128)}, u32[]{:S(2)}) copy-start(f32[16,32,256]{2,1,0:T(8,128)} %param.8) | copy-start | bytes 1572868
  12.0 31.9 %all-to-all-start = ((f32[16,2,16,256]{3,1,2,0:T(2,128)}), f32[16,2,16,256]{3,1,2,0:T(2,128)S(1)}, u32[]{:S(2)}, u32[]{:S(2)}) async-start(f32[16,2,16,256]{3,1,2,0:T(2,128)} %fusion.43), calls=%async_computation | async-start | bytes 1048576 | tf_op jit(solution)/shard_map/all_to_all | solution.py:48
  20.7 15.3 %collective-permute-start.4 = (f32[3,32,8]{2,1,0:T(8,128)S(1)}, f32[3,32,8]{2,1,0:T(8,128)S(1)}, u32[]{:S(2)}, u32[]{:S(2)}) collective-permute-start(f32[3,32,8]{2,1,0:T(8,128)S(1)} %get-tuple-element.13), channel_id=1, source_target_pairs={{0,16},{16,32},{32,48},{48,64},{64,80},{80,96},{96,112},{112,128},... | collective-permute-start | bytes 9224 | tf_op jit(solution)/shard_map/ppermute | solution.py:15
  21.1 14.9 %collective-permute-start.5 = (f32[3,32,8]{2,1,0:T(8,128)S(1)}, f32[3,32,8]{2,1,0:T(8,128)S(1)}, u32[]{:S(2)}, u32[]{:S(2)}) collective-permute-start(f32[3,32,8]{2,1,0:T(8,128)S(1)} %get-tuple-element.14), channel_id=1, source_target_pairs={{16,0},{32,16},{48,32},{64,48},{80,64},{96,80},{112,96},{128,112},... | collective-permute-start | bytes 9224 | tf_op jit(solution)/shard_map/ppermute | solution.py:18
  36.1 4.7 %collective-permute-start.6 = (f32[3,8,272]{2,1,0:T(8,128)S(1)}, f32[3,8,272]{2,1,0:T(8,128)S(1)}, u32[]{:S(2)}, u32[]{:S(2)}) collective-permute-start(f32[3,8,272]{2,1,0:T(8,128)S(1)} %get-tuple-element.11), channel_id=1, source_target_pairs={{0,1},{1,2},{2,3},{3,4},{4,5},{5,6},{6,7},{7,8},{8,9},{9,10},{10,1... | collective-permute-start | bytes 78344 | tf_op jit(solution)/shard_map/ppermute | solution.py:15
  36.3 7.3 %collective-permute-start.7 = (f32[3,8,272]{2,1,0:T(8,128)S(1)}, f32[3,8,272]{2,1,0:T(8,128)S(1)}, u32[]{:S(2)}, u32[]{:S(2)}) collective-permute-start(f32[3,8,272]{2,1,0:T(8,128)S(1)} %get-tuple-element.12), channel_id=1, source_target_pairs={{1,0},{2,1},{3,2},{4,3},{5,4},{6,5},{7,6},{8,7},{9,8},{10,9},{11,1... | collective-permute-start | bytes 78344 | tf_op jit(solution)/shard_map/ppermute | solution.py:18
  101.3 7.0 %collective-permute-start = (f32[16,32,8]{2,1,0:T(8,128)S(1)}, f32[16,32,8]{2,1,0:T(8,128)S(1)}, u32[]{:S(2)}, u32[]{:S(2)}) collective-permute-start(f32[16,32,8]{2,1,0:T(8,128)S(1)} %get-tuple-element.7), channel_id=1, source_target_pairs={{0,16},{16,32},{32,48},{48,64},{64,80},{80,96},{96,112},{112,128},... | collective-permute-start | bytes 49160 | tf_op jit(solution)/shard_map/ppermute | solution.py:15
  101.3 7.0 %collective-permute-start.1 = (f32[16,32,8]{2,1,0:T(8,128)S(1)}, f32[16,32,8]{2,1,0:T(8,128)S(1)}, u32[]{:S(2)}, u32[]{:S(2)}) collective-permute-start(f32[16,32,8]{2,1,0:T(8,128)S(1)} %get-tuple-element.8), channel_id=1, source_target_pairs={{16,0},{32,16},{48,32},{64,48},{80,64},{96,80},{112,96},{128,112},... | collective-permute-start | bytes 49160 | tf_op jit(solution)/shard_map/ppermute | solution.py:18
  108.5 5.7 %collective-permute-start.2 = (f32[16,8,272]{2,1,0:T(8,128)S(1)}, f32[16,8,272]{2,1,0:T(8,128)S(1)}, u32[]{:S(2)}, u32[]{:S(2)}) collective-permute-start(f32[16,8,272]{2,1,0:T(8,128)S(1)} %get-tuple-element.5), channel_id=1, source_target_pairs={{0,1},{1,2},{2,3},{3,4},{4,5},{5,6},{6,7},{7,8},{8,9},{9,10},{10,1... | collective-permute-start | bytes 417800 | tf_op jit(solution)/shard_map/ppermute | solution.py:15
  109.3 9.0 %collective-permute-start.3 = (f32[16,8,272]{2,1,0:T(8,128)S(1)}, f32[16,8,272]{2,1,0:T(8,128)S(1)}, u32[]{:S(2)}, u32[]{:S(2)}) collective-permute-start(f32[16,8,272]{2,1,0:T(8,128)S(1)} %get-tuple-element.6), channel_id=1, source_target_pairs={{1,0},{2,1},{3,2},{4,3},{5,4},{6,5},{7,6},{8,7},{9,8},{10,9},{11,1... | collective-permute-start | bytes 417800 | tf_op jit(solution)/shard_map/ppermute | solution.py:18
